TPU v7x, 128 devices: a whole 4x4x4 slice. The times are simulated.
128 devices in a mesh: lat: 32 (over z, y, core), chan: 4 (over x).
Axes of the slice: x: 4, y: 4, z: 4, core: 2. Of those that a mesh axis runs over, the one named last changes fastest.
Arguments:
- field: bfloat16 [32, 3, 2, 512, 4096], P('chan', None, None, 'lat'), may hold values from -6 to 6
- mix_weight: bfloat16 [32, 32], replicated, may hold values from -1 to 1
- spectral_gain: float32 [32, 2048], P('chan'), may hold values from 0.05 to 1
- legendre: bfloat16 [2, 512, 512, 1024], P(None, 'lat'), may hold values from -0.25 to 0.25
- slot_mode: int32 [512], replicated, may hold values from 0 to 511, as said below
Outputs:
- layered: bfloat16 [32, 3, 2, 512, 4096], P('chan', None, None, 'lat')
Inputs may be any that keep to these rules, and one draw needn't show every extreme that they name: `slot_mode`: A permutation of the mode indices; slots 2 j and 2 j + 1 carry the modes k and 511 - k for some k, so the slots of every index of lat carry whole such pairs.
All inputs are finite; a program needn't handle non-finite values.
Results may differ from a plain program's by a relative error of at most 0.0085.
Values may be sent and summed in bfloat16 or wider, within the bound.
No kernel may reach another device: no remote copies, remote signals or barrier semaphores. Data moves between devices by JAX's collectives and lax.ppermute only.
A program may use at most 192 MiB of HBM per device.

v0:
```python
import math
import jax
import jax.numpy as jnp
from jax import lax
from jax.sharding import PartitionSpec as P


def local(field, mix_weight, spectral_gain, legendre, slot_mode, n_lat, n_chan):
    chans = field.shape[0]
    fields = field.shape[1]
    cycles = field.shape[3]
    points = field.shape[4]
    total_modes = slot_mode.shape[0]
    degrees = spectral_gain.shape[1]
    half_deg = degrees // 2
    step_size = degrees // total_modes
    period = points // math.gcd(points, step_size)
    devices = n_lat * n_chan
    per_dev = total_modes // devices
    lat_index = lax.axis_index("lat")
    chan_index = lax.axis_index("chan")
    row_count = chans * fields * 2 * cycles
    modes = (slot_mode * step_size).reshape(n_lat, n_chan, per_dev)
    modes = jnp.transpose(modes, (1, 0, 2)).reshape(devices, 1, per_dev)
    quarter = jnp.array([0, points // 4], jnp.int32).reshape(1, 2, 1)
    lanes = min(128, period)
    blocks = period // lanes
    scale = 2.0 * math.pi / points
    hi_turns = (
        modes[..., None] * (lax.iota(jnp.int32, blocks) * lanes) + quarter[..., None]
    ) % points
    lo_turns = modes[..., None] * lax.iota(jnp.int32, lanes) % points
    hi_angle = hi_turns.astype(jnp.float32) * scale
    lo_angle = lo_turns.astype(jnp.float32) * scale
    ca, sa = (jnp.cos(hi_angle)[..., None], jnp.sin(hi_angle)[..., None])
    cb, sb = (jnp.cos(lo_angle)[..., None, :], jnp.sin(lo_angle)[..., None, :])
    basis = (ca * cb - sa * sb).reshape(-1, period)
    fwd = (basis * math.sqrt(2.0 / points)).astype(jnp.bfloat16)
    ratio = math.sqrt(points / (2.0 * total_modes))
    if ratio == 2.0 ** round(math.log2(ratio)):
        fwd = lax.optimization_barrier(fwd)
        inv = fwd
    else:
        inv = (basis * math.sqrt(1.0 / total_modes)).astype(jnp.bfloat16)
        ratio = 1.0
    flat = field.reshape(-1, points)
    summed = flat[:, :period].astype(jnp.float32)
    for n in range(1, points // period):
        summed = summed + flat[:, n * period : (n + 1) * period].astype(jnp.float32)
    high = summed.astype(jnp.bfloat16)
    low = (summed - high.astype(jnp.float32)).astype(jnp.bfloat16)
    rows = jnp.concatenate([high, low], axis=1)
    spec_t = lax.dot_general(
        jnp.concatenate([fwd, fwd], axis=1),
        rows,
        (((1,), (1,)), ((), ())),
        preferred_element_type=jnp.float32,
    ).astype(jnp.bfloat16)
    sent = spec_t.reshape(devices, 2 * per_dev, row_count)
    got = lax.all_to_all(sent, ("chan", "lat"), 0, 0, tiled=True)
    got = got.reshape(n_chan, n_lat, 2, per_dev, chans, fields, 2, cycles)
    sign = jnp.array([[1.0, 1.0], [1.0, -1.0]], jnp.float32)
    weight = mix_weight.astype(jnp.float32).reshape(-1, n_chan, chans)
    mix_fold = sign[:, None, None, :, None] * jnp.transpose(weight, (0, 2, 1))[None, :, :, None, :]
    mix_fold = mix_fold.astype(jnp.bfloat16)
    folded = jnp.einsum(
        "pokhC,CLqskthr->sptqoLr", mix_fold, got, preferred_element_type=jnp.float32
    ).astype(jnp.bfloat16)
    folded = folded.reshape(per_dev, 2, fields, 2, -1, n_lat * cycles)
    leg = lax.dynamic_slice_in_dim(legendre, chan_index * per_dev, per_dev, 1)
    coefficients = jnp.einsum(
        "sptqor,psri->sptqoi", folded, leg, preferred_element_type=jnp.float32
    )
    all_gain = lax.all_gather(spectral_gain, "chan", axis=0, tiled=True)
    gain_par = jnp.transpose(all_gain.reshape(-1, half_deg, 2), (2, 0, 1))
    own_modes = lax.dynamic_slice_in_dim(
        modes.reshape(-1), (chan_index * n_lat + lat_index) * per_dev, per_dev, 0
    )
    degree = 2 * lax.iota(jnp.int32, half_deg)[None, :] + lax.iota(jnp.int32, 2)[:, None]
    allowed = degree[None, :, :] >= own_modes[:, None, None]
    sign = jnp.array([[1.0, 1.0], [1.0, -1.0]], jnp.float32).reshape(1, 2, 2, 1, 1, 1, 1)
    scaled = gain_par[None, :, None, None, :, :] * coefficients
    filtered = jnp.where(
        allowed[:, None, :, None, None, None, :], sign * scaled[:, None], 0.0
    ).astype(jnp.bfloat16)
    back = jnp.einsum(
        "shptqoi,psri->shtqor", filtered, leg, preferred_element_type=jnp.float32
    ).astype(jnp.bfloat16)
    back = back.reshape(per_dev, 2, fields, 2, n_chan, chans, n_lat, cycles)
    leaving = jnp.transpose(back, (4, 6, 3, 0, 5, 2, 1, 7)).reshape(devices, 2 * per_dev, row_count)
    returned = lax.all_to_all(leaving, ("chan", "lat"), 0, 0, tiled=True)
    returned = returned.reshape(2 * total_modes, row_count)
    waveform = (
        lax.dot_general(returned, inv, (((0,), (0,)), ((), ())), preferred_element_type=jnp.float32)
        * ratio
    )
    waveform = waveform.reshape(chans, fields, -1, period)
    primal_h = waveform[:, 0]
    sigmoid_h = jax.nn.sigmoid(primal_h)
    slope_h = sigmoid_h * (1.0 + primal_h * (1.0 - sigmoid_h))
    gain_h = primal_h * sigmoid_h
    flat = field.reshape(chans, fields, -1, points)
    pieces = []
    for n in range(points // period):
        initial = flat[:, :, :, n * period : (n + 1) * period].astype(jnp.float32)
        primal = initial[:, 0] + gain_h
        tangents = initial[:, 1:] + slope_h[:, None] * waveform[:, 1:]
        pieces.append(jnp.concatenate([primal[:, None], tangents], axis=1).astype(jnp.bfloat16))
    out = jnp.concatenate(pieces, axis=3)
    return out.reshape(field.shape)


def solution(mesh):
    n_lat = mesh.shape["lat"]
    n_chan = mesh.shape["chan"]
    placed = (
        P("chan", None, None, "lat", None),
        P(),
        P("chan", None),
        P(None, "lat", None, None),
        P(),
    )

    def body(field, mix_weight, spectral_gain, legendre, slot_mode):
        return local(field, mix_weight, spectral_gain, legendre, slot_mode, n_lat, n_chan)

    return jax.shard_map(
        body,
        mesh=mesh,
        in_specs=placed,
        out_specs=P("chan", None, None, "lat", None),
        check_vma=False,
    )
```

profile of v0, /device:TPU:1, one launch (start us, length us, event | category | flops | bytes accessed | tf_op | source)
XLA Modules:
  0.0 178.5 jit_solution(10418024160867076549)
XLA Ops:
  0.0 0.7 broadcast_multiply_fusion.2
  0.7 0.1 reshape.164
  0.8 0.1 copy.57
  0.9 0.1 mul.227
  1.0 0.1 copy.59
  1.1 0.1 broadcast_multiply_fusion.1
  1.2 2.4 %fusion.54 = (f32[128,4,128]{2,1,0:T(4,128)S(1)}, f32[128,4,128]{2,1,0:T(4,128)S(1)}) fusion(s32[128,4]{1,0:T(8,128)S(1)} %copy.59), kind=kLoop, calls=%fused_computation.66 | loop fusion | flops 917504 | bytes 526336 | tf_op jit(solution)/shard_map/cos | solution.py:36
  3.6 0.2 fusion.63
  3.8 0.3 copy.58
  4.1 0.3 copy.60
  4.4 0.0 copy-start
  4.4 2.5 %multiply_convert_fusion = bf16[128,2,4,8,128]{4,3,2,1,0:T(8,128)(2,1)S(1)} fusion(f32[128,4,128]{2,1,0:T(4,128)S(1)} %get-tuple-element.21, f32[128,2,4,8]{3,2,1,0:T(4,128)S(1)} %copy.60, f32[128,4,128]{2,1,0:T(4,128)S(1)} %get-tuple-element.20, f32[128,2,4,8]{3,2,1,0:T(4,128)S(1)} %copy.58), kind=kLoop, calls=%fused_computation.21 | loop fusion | flops 5242880 | bytes 2686976 | tf_op jit(solution)/shard_map/convert_element_type | solution.py:38
  6.9 0.6 copy.103
  7.5 0.0 copy-start.4
  7.5 0.0 copy-done
  7.5 1.6 subtract_convert_fusion
  9.1 0.2 copy-done.4
  9.3 4.6 %fusion.39 = bf16[128,8,768]{2,1,0:T(8,128)(2,1)} fusion(bf16[768,1024]{1,0:T(8,128)(2,1)S(1)} %get-tuple-element.5, bf16[768,1024]{1,0:T(8,128)(2,1)S(1)} %get-tuple-element.6, bf16[1024,1024]{1,0:T(8,128)(2,1)S(1)} %bitcast.84), kind=kOutput, calls=%fused_computation.46 | convolution fusion | flops 3236691968 | bytes 6815744 | tf_op jit(solution)/shard_map/dot_general | solution.py:53
  13.9 11.5 %all-to-all-start = ((bf16[128,8,768]{2,1,0:T(8,128)(2,1)}), bf16[128,8,768]{2,1,0:T(8,128)(2,1)S(1)}, u32[]{:S(2)}, u32[]{:S(2)}) async-start(bf16[128,8,768]{2,1,0:T(8,128)(2,1)} %fusion.39), calls=%async_computation | async-start | bytes 3145728 | tf_op jit(solution)/shard_map/all_to_all | solution.py:60
  25.4 0.0 copy-done.6
  25.5 0.1 copy.62
  25.6 0.1 reshape_reshape.3
  25.7 0.0 copy-done.5
  25.7 25.3 %all_gather.3 = f32[32,2048]{1,0:T(8,128)S(1)} all-gather(f32[8,2048]{1,0:T(8,128)S(1)} %copy-done.5), channel_id=1, replica_groups=mesh['lat'=32,'chan'=4] {'chan'}, dimensions={0}, use_global_device_ids=true | all-gather | bytes 327680 | tf_op jit(solution)/shard_map/all_gather | solution.py:74
  51.0 0.3 copy.55
  51.3 0.4 copy.56
  51.8 0.1 dynamic_slice.6
  51.9 0.1 broadcast_compare_fusion
  52.0 0.0 all-to-all-done
  52.0 1.2 copy.61
  53.1 0.0 copy-start.7
  53.2 4.6 %reshape.168 = bf16[4,32,2,4,8,3,2,16]{1,0,7,6,5,4,3,2:T(4,128)(2,1)} reshape(bf16[128,8,768]{0,2,1:T(8,128)(2,1)S(1)} %copy.61) | data formatting | bytes 3145728 | tf_op jit(solution)/shard_map/reshape | solution.py:61
  57.8 9.6 %fusion.6 = bf16[4,2,3,2,32,32,16]{4,5,1,6,2,0,3:T(8,128)(2,1)} fusion(f32[32,8,4]{0,2,1:T(4,128)S(1)} %copy.63, f32[2,2]{1,0:T(2,128)S(1)} %copy-done.7, bf16[4,32,2,4,8,3,2,16]{1,0,7,6,5,4,3,2:T(4,128)(2,1)} %reshape.168), kind=kOutput, calls=%fused_computation.8 | convolution fusion | flops 101457920 | bytes 3149840 | tf_op jit(solution)/shard_map/pokhC,CLqskthr->sptqoLr/dot_general | solution.py:66
  67.3 10.1 %copy.65 = bf16[4,2,3,2,32,32,16]{4,6,5,3,2,1,0:T(8,128)(2,1)S(1)} copy(bf16[4,2,3,2,32,32,16]{4,5,1,6,2,0,3:T(8,128)(2,1)} %fusion.6) | data formatting | bytes 3145728 | tf_op jit(solution)/shard_map/convert_element_type | solution.py:68
  77.4 8.6 %broadcast_multiply_fusion = f32[4,2,3,2,32,1024]{5,4,1,3,2,0:T(8,128)} fusion(f32[2,32,1024]{2,1,0:T(8,128)S(1)} %copy.56, bf16[4,2,3,2,32,512]{4,5,3,2,1,0:T(8,128)(2,1)S(1)} %bitcast.80, bf16[2,16,512,1024]{3,2,1,0:T(8,128)(2,1)} %param.11, s32[]{:T(128)S(6)} %select_n.43), kind=kOutput, calls=%fused_computation.28 | convolution fusion | flops 1612185600 | bytes 16515076 | tf_op jit(solution)/shard_map/sptqor,psri->sptqoi/dot_general | solution.py:71
  86.0 8.7 %bitcast_convert_fusion.1 = bf16[4,2,3,2,32,512]{5,4,3,2,1,0:T(8,128)(2,1)S(1)} fusion(f32[4,2,3,2,32,1024]{5,4,1,3,2,0:T(8,128)} %broadcast_multiply_fusion, f32[2,2]{1,0:T(2,128)S(1)} %copy-done.7, pred[4,2,1024]{2,1,0:T(4,128)(4,1)S(1)} %broadcast_compare_fusion, bf16[2,16,512,1024]{3,2,1,0:T(8,128)(2,1)} %param.11, s32[]{:T(128)S(6)} %select_n.43), kind=kOutput, calls=%fused_computation.25 | convolution fusion | flops 3231449088 | bytes 16261140 | tf_op jit(solution)/shard_map/shptqoi,psri->shtqor/dot_general | solution.py:86
  94.7 11.9 %reshape.171 = bf16[4,2,3,2,4,8,32,16]{7,6,5,4,3,2,1,0:T(8,128)(2,1)} reshape(bf16[4,2,3,2,32,512]{5,4,3,2,1,0:T(8,128)(2,1)S(1)} %bitcast_convert_fusion.1) | data formatting | bytes 3145728 | tf_op jit(solution)/shard_map/reshape | solution.py:89
  106.5 14.5 %copy.68 = bf16[4,32,2,4,8,3,2,16]{1,0,7,6,5,4,3,2:T(4,128)(2,1)} copy(bf16[4,32,2,4,8,3,2,16]{7,1,4,0,2,5,6,3:T(8,128)(2,1)} %bitcast.77) | data formatting | bytes 3145728 | tf_op jit(solution)/shard_map/transpose | solution.py:90
  121.0 7.3 %reshape.172 = bf16[128,8,768]{0,2,1:T(8,128)(2,1)S(1)} reshape(bf16[4,32,2,4,8,3,2,16]{1,0,7,6,5,4,3,2:T(4,128)(2,1)} %copy.68) | data formatting | bytes 3145728 | tf_op jit(solution)/shard_map/reshape | solution.py:90
  128.3 2.0 %copy.69 = bf16[128,8,768]{2,1,0:T(8,128)(2,1)} copy(bf16[128,8,768]{0,2,1:T(8,128)(2,1)S(1)} %reshape.172) | data formatting | bytes 3145728 | tf_op jit(solution)/shard_map/reshape | solution.py:90
  130.3 10.3 %all-to-all-start.1 = ((bf16[128,8,768]{2,1,0:T(8,128)(2,1)}), bf16[128,8,768]{2,1,0:T(8,128)(2,1)}, u32[]{:S(2)}, u32[]{:S(2)}) async-start(bf16[128,8,768]{2,1,0:T(8,128)(2,1)} %copy.69), calls=%async_computation.1 | async-start | bytes 3145728 | tf_op jit(solution)/shard_map/all_to_all | solution.py:91
  140.6 7.2 %slice_convert_fusion.3 = (f32[8,3,32,1024]{3,2,1,0:T(8,128)S(1)}, f32[8,3,32,1024]{3,2,1,0:T(8,128)}, f32[8,3,32,1024]{3,2,1,0:T(8,128)}, f32[8,3,32,1024]{3,2,1,0:T(8,128)}) fusion(bf16[8,3,32,4096]{3,2,1,0:T(8,128)(2,1)} %bitcast.78), kind=kLoop, calls=%fused_computation.44 | loop fusion | flops 3145728 | bytes 18874368 | tf_op jit(solution)/shard_map/convert_element_type | solution.py:105
  147.8 17.2 %all-to-all-done.1 = bf16[128,8,768]{2,1,0:T(8,128)(2,1)} async-done(((bf16[128,8,768]{2,1,0:T(8,128)(2,1)}), bf16[128,8,768]{2,1,0:T(8,128)(2,1)}, u32[]{:S(2)}, u32[]{:S(2)}) %all-to-all-start.1) | async-done | bytes 1572896 | tf_op jit(solution)/shard_map/all_to_all | solution.py:91
  165.0 4.1 %convolution_multiply_fusion = f32[768,1024]{1,0:T(8,128)S(1)} fusion(bf16[1024,1024]{1,0:T(8,128)(2,1)} %bitcast.85, bf16[128,8,768]{2,1,0:T(8,128)(2,1)} %all-to-all-done.1), kind=kOutput, calls=%fused_computation.39 | convolution fusion | flops 1611399168 | bytes 6815744 | tf_op jit(solution)/shard_map/dot_general | solution.py:94
  169.1 3.1 %fusion.47 = (bf16[8,1,32,1024]{3,2,1,0:T(8,128)(2,1)S(1)}, bf16[8,1,32,1024]{3,2,1,0:T(8,128)(2,1)S(1)}, bf16[8,1,32,1024]{3,2,1,0:T(8,128)(2,1)}, bf16[8,1,32,1024]{3,2,1,0:T(8,128)(2,1)}, f32[8,32,1024]{2,1,0:T(8,128)S(1)}) fusion(f32[8,3,32,1024]{3,2,1,0:T(8,128)S(1)} %get-tuple-element.7, f32[8,3,32,1024]{3,2,1,0:T(8,128)S(1)} %bitcast.81, ...), kind=kLoop, calls=%fused_computation.54 | loop fusion | flops 4194304 | bytes 8388608 | tf_op jit(solution)/shard_map/convert.17
  172.3 0.0 copy-done.3
  172.3 1.7 fusion.30
  173.9 4.6 %maximum_maximum_fusion = bf16[8,3,2,16,4096]{4,3,2,1,0:T(8,128)(2,1)} fusion(bf16[8,2,2,16,1024]{4,3,2,1,0:T(8,128)(2,1)S(1)} %bitcast.90, bf16[8,1,2,16,1024]{4,3,2,1,0:T(8,128)(2,1)} %bitcast.94, bf16[8,2,2,16,1024]{4,3,2,1,0:T(8,128)(2,1)S(1)} %bitcast.89, bf16[8,1,2,16,1024]{4,3,2,1,0:T(8,128)(2,1)} %bitcast.93, ...), kind=kLoop, calls=%fused_computation.9 | loop fusion | flops 50331648 | bytes 12582912 | tf_op jit(solution)/shard_map/concatenate | solution.py:109
  (15 shorter events, 0.1 us)
Async XLA Ops:
  4.4 3.1 %copy-start = (bf16[8,3,2,16,4096]{4,3,2,1,0:T(8,128)(2,1)S(1)}, bf16[8,3,2,16,4096]{4,3,2,1,0:T(8,128)(2,1)}, u32[]{:S(2)}) copy-start(bf16[8,3,2,16,4096]{4,3,2,1,0:T(8,128)(2,1)} %param.8) | copy-start | bytes 18874372
  7.5 1.8 %copy-start.4 = (bf16[128,8,8,128]{3,1,2,0:T(8,128)(2,1)}, bf16[128,8,8,128]{3,1,2,0:T(8,128)(2,1)S(1)}, u32[]{:S(2)}) copy-start(bf16[128,8,8,128]{3,1,2,0:T(8,128)(2,1)S(1)} %copy.103) | copy-start | bytes 6291460
  9.3 16.1 %copy-start.6 = (bf16[32,32]{1,0:T(8,128)(2,1)S(1)}, bf16[32,32]{1,0:T(8,128)(2,1)}, u32[]{:S(2)}) copy-start(bf16[32,32]{1,0:T(8,128)(2,1)} %param.9) | copy-start | bytes 6148
  9.3 16.4 %copy-start.5 = (f32[8,2048]{1,0:T(8,128)S(1)}, f32[8,2048]{1,0:T(8,128)}, u32[]{:S(2)}) copy-start(f32[8,2048]{1,0:T(8,128)} %param.10) | copy-start | bytes 196612
  13.9 38.0 %all-to-all-start = ((bf16[128,8,768]{2,1,0:T(8,128)(2,1)}), bf16[128,8,768]{2,1,0:T(8,128)(2,1)S(1)}, u32[]{:S(2)}, u32[]{:S(2)}) async-start(bf16[128,8,768]{2,1,0:T(8,128)(2,1)} %fusion.39), calls=%async_computation | async-start | bytes 3145728 | tf_op jit(solution)/shard_map/all_to_all | solution.py:60
  53.1 4.6 %copy-start.7 = (f32[2,2]{1,0:T(2,128)S(1)}, f32[2,2]{1,0:T(2,128)}, u32[]{:S(2)}) copy-start(f32[2,2]{1,0:T(2,128)} %constant.63.clone) | copy-start | bytes 52
  130.3 34.7 %all-to-all-start.1 = ((bf16[128,8,768]{2,1,0:T(8,128)(2,1)}), bf16[128,8,768]{2,1,0:T(8,128)(2,1)}, u32[]{:S(2)}, u32[]{:S(2)}) async-start(bf16[128,8,768]{2,1,0:T(8,128)(2,1)} %copy.69), calls=%async_computation.1 | async-start | bytes 3145728 | tf_op jit(solution)/shard_map/all_to_all | solution.py:91
  165.0 4.1 %copy-start.1 = (f32[8,3,32,1024]{3,2,1,0:T(8,128)S(1)}, f32[8,3,32,1024]{3,2,1,0:T(8,128)}, u32[]{:S(2)}) copy-start(f32[8,3,32,1024]{3,2,1,0:T(8,128)} %get-tuple-element.8) | copy-start | bytes 9437188
  165.0 4.1 %copy-start.2 = (f32[8,3,32,1024]{3,2,1,0:T(8,128)S(1)}, f32[8,3,32,1024]{3,2,1,0:T(8,128)}, u32[]{:S(2)}) copy-start(f32[8,3,32,1024]{3,2,1,0:T(8,128)} %get-tuple-element.9) | copy-start | bytes 9437188
  169.1 3.2 %copy-start.3 = (f32[8,3,32,1024]{3,2,1,0:T(8,128)S(1)}, f32[8,3,32,1024]{3,2,1,0:T(8,128)}, u32[]{:S(2)}) copy-start(f32[8,3,32,1024]{3,2,1,0:T(8,128)} %get-tuple-element.10) | copy-start | bytes 9437188
where the time goes:
time: 179 us
  local copies, waits for them, and re-layouts  54.3 us (30%)
  matrix products  35.5 us (20%)
  blocking collectives  25.3 us (14%)
  other arithmetic  24.1 us (13%)
  starting transfers between devices  21.8 us (12%)
  waiting for transfers between devices  17.2 us (10%)
    all_gather x1, blocking collectives, local(): all_gain = lax.all_gather(spectral_gain, 'chan', axis=0, tiled=True)  25.3 us
    all_to_all x1, waiting for transfers between devices, local(): returned = lax.all_to_all(leaving, ('chan', 'lat'), 0, 0, tiled=True)  17.2 us
    transpose x1, local copies, waits for them, and re-layouts, local(): jnp.transpose(back, (4, 6, 3, 0, 5, 2, 1, 7))  14.5 us
    reshape x1, local copies, waits for them, and re-layouts, local(): back = back.reshape(per_dev, 2, fields, 2, n_chan, chans, n_lat, cycles)  11.9 us
    all_to_all x1, starting transfers between devices, local(): got = lax.all_to_all(sent, ('chan', 'lat'), 0, 0, tiled=True)  11.5 us
    all_to_all x1, starting transfers between devices, local(): returned = lax.all_to_all(leaving, ('chan', 'lat'), 0, 0, tiled=True)  10.3 us
    convert_element_type x1, local copies, waits for them, and re-layouts, local(): folded = jnp.einsum('pokhC,CLqskthr->sptqoLr', mix_fold, got, preferred_e...  10.1 us
    dot_general x1, matrix products, local(): jnp.einsum('pokhC,CLqskthr->sptqoLr', mix_fold, got, preferred_element_ty...  9.56 us
  transfers between devices with their start and end apart: 2, of which 1 were waited for; matrix products, arithmetic and copies ran while one was open for 5% of the time, Pallas kernels for 0%

commit v1 on v0

--- a/solution.py
+++ b/solution.py
@@ -3,9 +3,16 @@
 import jax.numpy as jnp
 from jax import lax
 from jax.sharding import PartitionSpec as P
+from jax.lax import all_to_all, axis_size
 
 
 def local(field, mix_weight, spectral_gain, legendre, slot_mode, n_lat, n_chan):
+
+    def point_the_plane(mine_x, d_out):
+        a_next = jnp.stack([mine_x] * axis_size("chan"))
+        long_array = all_to_all(a_next, split_axis=0, concat_axis=0, axis_name="chan")
+        return jnp.concatenate(long_array, axis=d_out)
+
     chans = field.shape[0]
     fields = field.shape[1]
     cycles = field.shape[3]
@@ -71,7 +78,7 @@
     coefficients = jnp.einsum(
         "sptqor,psri->sptqoi", folded, leg, preferred_element_type=jnp.float32
     )
-    all_gain = lax.all_gather(spectral_gain, "chan", axis=0, tiled=True)
+    all_gain = point_the_plane(spectral_gain, d_out=0)
     gain_par = jnp.transpose(all_gain.reshape(-1, half_deg, 2), (2, 0, 1))
     own_modes = lax.dynamic_slice_in_dim(
         modes.reshape(-1), (chan_index * n_lat + lat_index) * per_dev, per_dev, 0

time: 179 us -> 180 us (level)
  blocking collectives: 25.3 us -> 0 us
  waiting for transfers between devices: 17.2 us -> 33.9 us
  local copies, waits for them, and re-layouts: 54.3 us -> 62.9 us
    all_gather x1 -> x0, blocking collectives: 25.3 us -> none  [local(): all_gain = lax.all_gather(spectral_gain, 'chan', axis=0, tiled=True)]
    all_to_all x1, waiting for transfers between devices: 0.01 us -> 16.5 us  [local(): got = lax.all_to_all(sent, ('chan', 'lat'), 0, 0, tiled=True)]
    another operation x0 -> x2, local copies, waits for them, and re-layouts: none -> 5.84 us  [the longest x1 4.28 us: local(): gain_par = jnp.transpose(all_gain.reshape(-1, half_deg, 2), (2, 0, 1))]
    all_to_all x0 -> x1, starting transfers between devices: none -> 4.84 us  [point_the_plane(): all_to_all(a_next, split_axis=0, concat_axis=0, axis_name='chan')]
    all_to_all x1, starting transfers between devices: 10.3 us -> 5.6 us  [local(): returned = lax.all_to_all(leaving, ('chan', 'lat'), 0, 0, tiled=True)]
    all_to_all x0 -> x1, local copies, waits for them, and re-layouts: none -> 3 us  [point_the_plane(): all_to_all(a_next, split_axis=0, concat_axis=0, axis_name='chan')]
  transfers between devices with their start and end apart: 2 -> 3, of which waited for: 1 -> 2; matrix products, arithmetic and copies ran while one was open for 5% -> 16% of each run, Pallas kernels for 0% -> 0%
where the time goes in v1:
time: 180 us; the launch traced here: 178 us
  local copies, waits for them, and re-layouts  62.9 us (35%)
  matrix products  35.5 us (20%)
  waiting for transfers between devices  33.9 us (19%)
  other arithmetic  24.1 us (13%)
  starting transfers between devices  21.9 us (12%)
    all_to_all x1, waiting for transfers between devices, local(): returned = lax.all_to_all(leaving, ('chan', 'lat'), 0, 0, tiled=True)  17.3 us
    all_to_all x1, waiting for transfers between devices, local(): got = lax.all_to_all(sent, ('chan', 'lat'), 0, 0, tiled=True)  16.5 us
    transpose x1, local copies, waits for them, and re-layouts, local(): jnp.transpose(back, (4, 6, 3, 0, 5, 2, 1, 7))  14.5 us
    reshape x1, local copies, waits for them, and re-layouts, local(): back = back.reshape(per_dev, 2, fields, 2, n_chan, chans, n_lat, cycles)  11.9 us
    all_to_all x1, starting transfers between devices, local(): got = lax.all_to_all(sent, ('chan', 'lat'), 0, 0, tiled=True)  11.5 us
    convert_element_type x1, local copies, waits for them, and re-layouts, local(): folded = jnp.einsum('pokhC,CLqskthr->sptqoLr', mix_fold, got, preferred_e...  10.1 us
    dot_general x1, matrix products, local(): jnp.einsum('pokhC,CLqskthr->sptqoLr', mix_fold, got, preferred_element_ty...  9.56 us
    reshape x2, local copies, waits for them, and re-layouts, local(): jnp.transpose(back, (4, 6, 3, 0, 5, 2, 1, 7))  9.33 us
  transfers between devices with their start and end apart: 3, of which 2 were waited for; matrix products, arithmetic and copies ran while one was open for 16% of the time, Pallas kernels for 0%

profile of v1, /device:TPU:1, one launch (start us, length us, event | category | flops | bytes accessed | tf_op | source)
XLA Modules:
  0.0 178.5 jit_solution(11095630476859552604)
XLA Ops:
  0.0 1.6 stack.2
  1.6 4.8 %all-to-all-start = ((f32[4,8,2048]{2,1,0:T(8,128)}), f32[4,8,2048]{2,1,0:T(8,128)S(1)}, u32[]{:S(2)}, u32[]{:S(2)}) async-start(f32[4,8,2048]{2,1,0:T(8,128)} %stack.2), calls=%async_computation | async-start | bytes 524288 | tf_op jit(solution)/shard_map/all_to_all | solution.py:13
  6.4 0.7 broadcast_multiply_fusion.2
  7.1 0.1 reshape.163
  7.2 0.1 copy.56
  7.3 0.1 mul.227
  7.4 0.1 copy.58
  7.5 0.1 broadcast_multiply_fusion.1
  7.6 2.4 %fusion.54 = (f32[128,4,128]{2,1,0:T(4,128)S(1)}, f32[128,4,128]{2,1,0:T(4,128)S(1)}) fusion(s32[128,4]{1,0:T(8,128)S(1)} %copy.58), kind=kLoop, calls=%fused_computation.66 | loop fusion | flops 917504 | bytes 526336 | tf_op jit(solution)/shard_map/cos | solution.py:43
  10.0 0.2 fusion.63
  10.2 0.3 copy.57
  10.5 0.3 copy.59
  10.8 0.0 copy-start
  10.8 2.5 %multiply_convert_fusion = bf16[128,2,4,8,128]{4,3,2,1,0:T(8,128)(2,1)S(1)} fusion(f32[128,4,128]{2,1,0:T(4,128)S(1)} %get-tuple-element.21, f32[128,2,4,8]{3,2,1,0:T(4,128)S(1)} %copy.59, f32[128,4,128]{2,1,0:T(4,128)S(1)} %get-tuple-element.20, f32[128,2,4,8]{3,2,1,0:T(4,128)S(1)} %copy.57), kind=kLoop, calls=%fused_computation.21 | loop fusion | flops 5242880 | bytes 2686976 | tf_op jit(solution)/shard_map/convert_element_type | solution.py:45
  13.3 0.6 copy.102
  13.9 0.0 copy-start.4
  13.9 0.0 copy-done
  13.9 1.6 subtract_convert_fusion
  15.5 0.2 copy-done.4
  15.7 4.6 %fusion.39 = bf16[128,8,768]{2,1,0:T(8,128)(2,1)} fusion(bf16[768,1024]{1,0:T(8,128)(2,1)S(1)} %get-tuple-element.5, bf16[768,1024]{1,0:T(8,128)(2,1)S(1)} %get-tuple-element.6, bf16[1024,1024]{1,0:T(8,128)(2,1)S(1)} %bitcast.84), kind=kOutput, calls=%fused_computation.46 | convolution fusion | flops 3236691968 | bytes 6815744 | tf_op jit(solution)/shard_map/dot_general | solution.py:60
  20.3 0.0 all-to-all-done
  20.3 11.5 %all-to-all-start.1 = ((bf16[128,8,768]{2,1,0:T(8,128)(2,1)}), bf16[128,8,768]{2,1,0:T(8,128)(2,1)S(1)}, u32[]{:S(2)}, u32[]{:S(2)}) async-start(bf16[128,8,768]{2,1,0:T(8,128)(2,1)} %fusion.39), calls=%async_computation.1 | async-start | bytes 3145728 | tf_op jit(solution)/shard_map/all_to_all | solution.py:67
  31.8 0.1 copy.61
  31.9 0.1 reshape_reshape.6
  32.1 0.1 dynamic_slice.6
  32.1 0.1 broadcast_compare_fusion
  32.2 3.0 %copy.54 = f32[4,8,2048]{1,0,2:T(4,128)} copy(f32[4,8,2048]{2,1,0:T(8,128)S(1)} %all-to-all-done) | data formatting | bytes 524288 | tf_op jit(solution)/shard_map/all_to_all | solution.py:13
  35.2 4.3 %reshape_reshape.7 = f32[32,1024,2]{0,2,1:T(2,128)S(1)} reshape(f32[4,8,2048]{1,0,2:T(4,128)} %copy.54) | data formatting | bytes 524288 | tf_op jit(solution)/shard_map/reshape;reshape | solution.py:82
  39.5 0.4 copy.55
  40.0 16.5 %all-to-all-done.1 = bf16[128,8,768]{2,1,0:T(8,128)(2,1)S(1)} async-done(((bf16[128,8,768]{2,1,0:T(8,128)(2,1)}), bf16[128,8,768]{2,1,0:T(8,128)(2,1)S(1)}, u32[]{:S(2)}, u32[]{:S(2)}) %all-to-all-start.1) | async-done | bytes 1572896 | tf_op jit(solution)/shard_map/all_to_all | solution.py:67
  56.5 1.2 copy.60
  57.7 0.0 copy-start.6
  57.7 4.6 %reshape.166 = bf16[4,32,2,4,8,3,2,16]{1,0,7,6,5,4,3,2:T(4,128)(2,1)} reshape(bf16[128,8,768]{0,2,1:T(8,128)(2,1)S(1)} %copy.60) | data formatting | bytes 3145728 | tf_op jit(solution)/shard_map/reshape | solution.py:68
  62.3 9.6 %fusion.6 = bf16[4,2,3,2,32,32,16]{4,5,1,6,2,0,3:T(8,128)(2,1)} fusion(f32[32,8,4]{0,2,1:T(4,128)S(1)} %copy.62, f32[2,2]{1,0:T(2,128)S(1)} %copy-done.6, bf16[4,32,2,4,8,3,2,16]{1,0,7,6,5,4,3,2:T(4,128)(2,1)} %reshape.166), kind=kOutput, calls=%fused_computation.8 | convolution fusion | flops 101457920 | bytes 3149840 | tf_op jit(solution)/shard_map/pokhC,CLqskthr->sptqoLr/dot_general | solution.py:73
  71.9 10.1 %copy.64 = bf16[4,2,3,2,32,32,16]{4,6,5,3,2,1,0:T(8,128)(2,1)S(1)} copy(bf16[4,2,3,2,32,32,16]{4,5,1,6,2,0,3:T(8,128)(2,1)} %fusion.6) | data formatting | bytes 3145728 | tf_op jit(solution)/shard_map/convert_element_type | solution.py:75
  81.9 8.6 %broadcast_multiply_fusion = f32[4,2,3,2,32,1024]{5,4,1,3,2,0:T(8,128)} fusion(f32[2,32,1024]{2,1,0:T(8,128)S(1)} %copy.55, bf16[4,2,3,2,32,512]{4,5,3,2,1,0:T(8,128)(2,1)S(1)} %bitcast.80, bf16[2,16,512,1024]{3,2,1,0:T(8,128)(2,1)} %param.11, s32[]{:T(128)S(6)} %select_n.43), kind=kOutput, calls=%fused_computation.28 | convolution fusion | flops 1612185600 | bytes 16515076 | tf_op jit(solution)/shard_map/sptqor,psri->sptqoi/dot_general | solution.py:78
  90.5 8.7 %bitcast_convert_fusion.1 = bf16[4,2,3,2,32,512]{5,4,3,2,1,0:T(8,128)(2,1)S(1)} fusion(f32[4,2,3,2,32,1024]{5,4,1,3,2,0:T(8,128)} %broadcast_multiply_fusion, f32[2,2]{1,0:T(2,128)S(1)} %copy-done.6, pred[4,2,1024]{2,1,0:T(4,128)(4,1)S(1)} %broadcast_compare_fusion, bf16[2,16,512,1024]{3,2,1,0:T(8,128)(2,1)} %param.11, s32[]{:T(128)S(6)} %select_n.43), kind=kOutput, calls=%fused_computation.25 | convolution fusion | flops 3231449088 | bytes 16261140 | tf_op jit(solution)/shard_map/shptqoi,psri->shtqor/dot_general | solution.py:93
  99.2 11.9 %reshape.169 = bf16[4,2,3,2,4,8,32,16]{7,6,5,4,3,2,1,0:T(8,128)(2,1)} reshape(bf16[4,2,3,2,32,512]{5,4,3,2,1,0:T(8,128)(2,1)S(1)} %bitcast_convert_fusion.1) | data formatting | bytes 3145728 | tf_op jit(solution)/shard_map/reshape | solution.py:96
  111.0 14.5 %copy.67 = bf16[4,32,2,4,8,3,2,16]{1,0,7,6,5,4,3,2:T(4,128)(2,1)} copy(bf16[4,32,2,4,8,3,2,16]{7,1,4,0,2,5,6,3:T(8,128)(2,1)} %bitcast.77) | data formatting | bytes 3145728 | tf_op jit(solution)/shard_map/transpose | solution.py:97
  125.5 7.3 %reshape.170 = bf16[128,8,768]{0,2,1:T(8,128)(2,1)S(1)} reshape(bf16[4,32,2,4,8,3,2,16]{1,0,7,6,5,4,3,2:T(4,128)(2,1)} %copy.67) | data formatting | bytes 3145728 | tf_op jit(solution)/shard_map/reshape | solution.py:97
  132.8 2.0 %copy.68 = bf16[128,8,768]{2,1,0:T(8,128)(2,1)} copy(bf16[128,8,768]{0,2,1:T(8,128)(2,1)S(1)} %reshape.170) | data formatting | bytes 3145728 | tf_op jit(solution)/shard_map/reshape | solution.py:97
  134.8 5.6 %all-to-all-start.2 = ((bf16[128,8,768]{2,1,0:T(8,128)(2,1)}), bf16[128,8,768]{2,1,0:T(8,128)(2,1)}, u32[]{:S(2)}, u32[]{:S(2)}) async-start(bf16[128,8,768]{2,1,0:T(8,128)(2,1)} %copy.68), calls=%async_computation.2 | async-start | bytes 3145728 | tf_op jit(solution)/shard_map/all_to_all | solution.py:98
  140.5 7.2 %slice_convert_fusion.3 = (f32[8,3,32,1024]{3,2,1,0:T(8,128)S(1)}, f32[8,3,32,1024]{3,2,1,0:T(8,128)}, f32[8,3,32,1024]{3,2,1,0:T(8,128)}, f32[8,3,32,1024]{3,2,1,0:T(8,128)}) fusion(bf16[8,3,32,4096]{3,2,1,0:T(8,128)(2,1)} %bitcast.78), kind=kLoop, calls=%fused_computation.44 | loop fusion | flops 3145728 | bytes 18874368 | tf_op jit(solution)/shard_map/convert_element_type | solution.py:112
  147.6 17.3 %all-to-all-done.2 = bf16[128,8,768]{2,1,0:T(8,128)(2,1)} async-done(((bf16[128,8,768]{2,1,0:T(8,128)(2,1)}), bf16[128,8,768]{2,1,0:T(8,128)(2,1)}, u32[]{:S(2)}, u32[]{:S(2)}) %all-to-all-start.2) | async-done | bytes 1572896 | tf_op jit(solution)/shard_map/all_to_all | solution.py:98
  165.0 4.1 %convolution_multiply_fusion = f32[768,1024]{1,0:T(8,128)S(1)} fusion(bf16[1024,1024]{1,0:T(8,128)(2,1)} %bitcast.85, bf16[128,8,768]{2,1,0:T(8,128)(2,1)} %all-to-all-done.2), kind=kOutput, calls=%fused_computation.39 | convolution fusion | flops 1611399168 | bytes 6815744 | tf_op jit(solution)/shard_map/dot_general | solution.py:101
  169.1 3.1 %fusion.47 = (bf16[8,1,32,1024]{3,2,1,0:T(8,128)(2,1)S(1)}, bf16[8,1,32,1024]{3,2,1,0:T(8,128)(2,1)S(1)}, bf16[8,1,32,1024]{3,2,1,0:T(8,128)(2,1)}, bf16[8,1,32,1024]{3,2,1,0:T(8,128)(2,1)}, f32[8,32,1024]{2,1,0:T(8,128)S(1)}) fusion(f32[8,3,32,1024]{3,2,1,0:T(8,128)S(1)} %get-tuple-element.7, f32[8,3,32,1024]{3,2,1,0:T(8,128)S(1)} %bitcast.81, ...), kind=kLoop, calls=%fused_computation.54 | loop fusion | flops 4194304 | bytes 8388608 | tf_op jit(solution)/shard_map/convert.17
  172.2 1.7 fusion.30
  173.9 4.6 %maximum_maximum_fusion = bf16[8,3,2,16,4096]{4,3,2,1,0:T(8,128)(2,1)} fusion(bf16[8,2,2,16,1024]{4,3,2,1,0:T(8,128)(2,1)S(1)} %bitcast.90, bf16[8,1,2,16,1024]{4,3,2,1,0:T(8,128)(2,1)} %bitcast.94, bf16[8,2,2,16,1024]{4,3,2,1,0:T(8,128)(2,1)S(1)} %bitcast.89, bf16[8,1,2,16,1024]{4,3,2,1,0:T(8,128)(2,1)} %bitcast.93, ...), kind=kLoop, calls=%fused_computation.9 | loop fusion | flops 50331648 | bytes 12582912 | tf_op jit(solution)/shard_map/concatenate | solution.py:116
  (16 shorter events, 0.1 us)
Async XLA Ops:
  1.6 18.8 %all-to-all-start = ((f32[4,8,2048]{2,1,0:T(8,128)}), f32[4,8,2048]{2,1,0:T(8,128)S(1)}, u32[]{:S(2)}, u32[]{:S(2)}) async-start(f32[4,8,2048]{2,1,0:T(8,128)} %stack.2), calls=%async_computation | async-start | bytes 524288 | tf_op jit(solution)/shard_map/all_to_all | solution.py:13
  10.8 3.1 %copy-start = (bf16[8,3,2,16,4096]{4,3,2,1,0:T(8,128)(2,1)S(1)}, bf16[8,3,2,16,4096]{4,3,2,1,0:T(8,128)(2,1)}, u32[]{:S(2)}) copy-start(bf16[8,3,2,16,4096]{4,3,2,1,0:T(8,128)(2,1)} %param.8) | copy-start | bytes 18874372
  13.9 1.8 %copy-start.4 = (bf16[128,8,8,128]{3,1,2,0:T(8,128)(2,1)}, bf16[128,8,8,128]{3,1,2,0:T(8,128)(2,1)S(1)}, u32[]{:S(2)}) copy-start(bf16[128,8,8,128]{3,1,2,0:T(8,128)(2,1)S(1)} %copy.102) | copy-start | bytes 6291460
  15.7 16.1 %copy-start.5 = (bf16[32,32]{1,0:T(8,128)(2,1)S(1)}, bf16[32,32]{1,0:T(8,128)(2,1)}, u32[]{:S(2)}) copy-start(bf16[32,32]{1,0:T(8,128)(2,1)} %param.9) | copy-start | bytes 6148
  20.3 36.2 %all-to-all-start.1 = ((bf16[128,8,768]{2,1,0:T(8,128)(2,1)}), bf16[128,8,768]{2,1,0:T(8,128)(2,1)S(1)}, u32[]{:S(2)}, u32[]{:S(2)}) async-start(bf16[128,8,768]{2,1,0:T(8,128)(2,1)} %fusion.39), calls=%async_computation.1 | async-start | bytes 3145728 | tf_op jit(solution)/shard_map/all_to_all | solution.py:67
  57.7 4.6 %copy-start.6 = (f32[2,2]{1,0:T(2,128)S(1)}, f32[2,2]{1,0:T(2,128)}, u32[]{:S(2)}) copy-start(f32[2,2]{1,0:T(2,128)} %constant.63.clone) | copy-start | bytes 52
  134.8 30.1 %all-to-all-start.2 = ((bf16[128,8,768]{2,1,0:T(8,128)(2,1)}), bf16[128,8,768]{2,1,0:T(8,128)(2,1)}, u32[]{:S(2)}, u32[]{:S(2)}) async-start(bf16[128,8,768]{2,1,0:T(8,128)(2,1)} %copy.68), calls=%async_computation.2 | async-start | bytes 3145728 | tf_op jit(solution)/shard_map/all_to_all | solution.py:98
  165.0 4.1 %copy-start.1 = (f32[8,3,32,1024]{3,2,1,0:T(8,128)S(1)}, f32[8,3,32,1024]{3,2,1,0:T(8,128)}, u32[]{:S(2)}) copy-start(f32[8,3,32,1024]{3,2,1,0:T(8,128)} %get-tuple-element.8) | copy-start | bytes 9437188
  165.0 4.1 %copy-start.2 = (f32[8,3,32,1024]{3,2,1,0:T(8,128)S(1)}, f32[8,3,32,1024]{3,2,1,0:T(8,128)}, u32[]{:S(2)}) copy-start(f32[8,3,32,1024]{3,2,1,0:T(8,128)} %get-tuple-element.9) | copy-start | bytes 9437188
  169.1 3.1 %copy-start.3 = (f32[8,3,32,1024]{3,2,1,0:T(8,128)S(1)}, f32[8,3,32,1024]{3,2,1,0:T(8,128)}, u32[]{:S(2)}) copy-start(f32[8,3,32,1024]{3,2,1,0:T(8,128)} %get-tuple-element.10) | copy-start | bytes 9437188
